TPU v7x, 512 devices: a whole 4x8x8 slice. The times are simulated.
512 devices in a mesh: blk: 64 (over y_lo, z, core), tp: 8 (over y_hi, x).
Axes of the slice: x: 4, y: 8 (y_hi: 2, y_lo: 4; y = y_hi * 4 + y_lo), z: 8, core: 2. Of those that a mesh axis runs over, the one named last changes fastest.
Arguments:
- embeds: bfloat16 [8192, 5120], P('blk', 'tp')
- given_embeds: bfloat16 [8192, 5120], P('blk', 'tp')
- accept: int32 [8192], P('blk'), may hold values 0 or 1
- lengths: int32 [64], P('blk'), may hold values from 4 to 4096, as said below
- block_keep: int32 [64, 64], P('blk'), may hold values from 0 to 1
- norm_gain: bfloat16 [5120], replicated, may hold values from 0.25 to 1.75
- w_query: bfloat16 [5120, 5120], P('blk', 'tp'), may hold values from -0.078125 to 0.078125
- b_query: bfloat16 [5120], P('tp'), may hold values from -4 to 4
- w_key: bfloat16 [5120, 1024], P('blk', 'tp'), may hold values from -0.078125 to 0.078125
- b_key: bfloat16 [1024], P('tp'), may hold values from -4 to 4
- w_value: bfloat16 [5120, 1024], P('blk', 'tp'), may hold values from -0.078125 to 0.078125
- b_value: bfloat16 [1024], P('tp'), may hold values from -4 to 4
- cache_keys: bfloat16 [4096, 1024], P('blk', 'tp'), as said below
- cache_values: bfloat16 [4096, 1024], P('blk', 'tp'), may hold values from -6 to 6
Outputs:
- first_pass: bfloat16 [8192, 5120], P('blk', 'tp')
- second_pass: bfloat16 [8192, 5120], P('blk', 'tp')
Inputs may be any that keep to these rules, and one draw needn't show every extreme that they name: `lengths`: every request sees at least the first 4 prompt positions; some request sees all 4096. `cache_keys`: entries lie between -160 and 160.
All inputs are finite; a program needn't handle non-finite values. No bound on the sum of `accept` on one device may be relied on, other than what follows from the above.
Results may differ from a plain program's by a relative error of at most 0.012.
The roundings to bfloat16 on the way count: a program that leaves them out, or rounds other values in their place, can miss the bound.
Values may be sent and summed in bfloat16 or wider, within the bound.
No kernel may reach another device: no remote copies, remote signals or barrier semaphores. Data moves between devices by JAX's collectives and lax.ppermute only.
A program may use at most 64 MiB of HBM per device.

v0:
```python
import math
import jax
import jax.numpy as jnp
from jax import lax
from jax.sharding import PartitionSpec as P

KVH = 8
HD = 128
HQ = 40
CB = 64


def rotate(vectors, positions):
    halfway = HD // 2
    frequency = 1000000.0 ** (-(jnp.arange(halfway, dtype=jnp.float32) * (2.0 / HD)))
    angles = positions[..., None] * frequency
    cosine = jnp.cos(angles)[..., None, :]
    sine_part = jnp.sin(angles)[..., None, :]
    front_part = vectors[..., :halfway]
    back_part = vectors[..., halfway:]
    return jnp.concatenate(
        [front_part * cosine - back_part * sine_part, back_part * cosine + front_part * sine_part],
        axis=-1,
    )


def normalize(rows_in, norm_gain):
    widened = rows_in.astype(jnp.float32)
    inverse = lax.rsqrt(jnp.mean(widened * widened, axis=-1, keepdims=True) + 1e-06)
    return (widened * inverse * norm_gain.astype(jnp.float32)).astype(jnp.bfloat16)


def local(
    embeds,
    given_embeds,
    accept,
    lengths,
    block_keep,
    norm_gain,
    w_query,
    b_query,
    w_key,
    b_key,
    w_value,
    b_value,
    cache_keys,
    cache_values,
):
    grouping = HQ // KVH
    local_kv = w_key.shape[1] // HD
    local_q = local_kv * grouping
    block_rows = embeds.shape[0]
    blocks_all = block_keep.shape[1]
    inv_root = 1.0 / math.sqrt(HD)
    first_rows, given_rows = (
        lax.all_gather(embeds, "tp", axis=1, tiled=True),
        lax.all_gather(given_embeds, "tp", axis=1, tiled=True),
    )
    revised = jnp.where(accept[:, None] == 1, given_rows, first_rows)
    normed = normalize(jnp.concatenate([first_rows, revised], axis=0), norm_gain)
    pieces = (
        lax.all_gather(w_query, "blk", axis=0, tiled=True),
        lax.all_gather(w_key, "blk", axis=0, tiled=True),
        lax.all_gather(w_value, "blk", axis=0, tiled=True),
    )
    queries, key_proj, value_proj = tuple(
        (
            jnp.dot(normed, weight_piece, preferred_element_type=jnp.float32)
            for weight_piece in pieces
        )
    )
    queries = queries + b_query.astype(jnp.float32)
    key_proj = key_proj + b_key.astype(jnp.float32)
    value_proj = value_proj + b_value.astype(jnp.float32)
    length = lengths[0]
    keep_row = block_keep[0]
    positions = length.astype(jnp.float32) + jnp.arange(block_rows, dtype=jnp.float32)
    q_rot = rotate(queries.reshape(2, block_rows, local_q, HD), positions).astype(jnp.bfloat16)
    q_rot = q_rot.reshape(2, block_rows, local_kv, grouping, HD)
    k_rot = rotate(key_proj.reshape(2, block_rows, local_kv, HD), positions).astype(jnp.bfloat16)
    value_rows = value_proj.astype(jnp.bfloat16).reshape(2, block_rows, local_kv, HD)
    own_scores = (
        jnp.einsum("pqkgd,pjkd->pkgqj", q_rot, k_rot, preferred_element_type=jnp.float32) * inv_root
    )
    highest = jnp.max(own_scores, axis=-1)
    own_weights = jnp.exp(own_scores - highest[..., None])
    totals = jnp.sum(own_weights, axis=-1)
    mixture = jnp.einsum(
        "pkgqj,pjkd->pkgqd",
        own_weights.astype(jnp.bfloat16),
        value_rows,
        preferred_element_type=jnp.float32,
    )
    running = (highest, totals, mixture)
    key_piece = lax.all_gather(cache_keys, "blk", axis=0, tiled=True)
    value_piece = lax.all_gather(cache_values, "blk", axis=0, tiled=True)
    piece_rows = key_piece.shape[0]
    sub_rows = math.gcd(piece_rows, CB)
    count = piece_rows // sub_rows
    key_blocks = key_piece.reshape(count, sub_rows, local_kv, HD)
    value_blocks = value_piece.reshape(count, sub_rows, local_kv, HD)
    block_starts = jnp.arange(count, dtype=jnp.int32) * sub_rows

    def visit(running_now, inputs):
        key_rows, value_block, position = inputs
        cache_index = position + jnp.arange(sub_rows, dtype=jnp.int32)
        block_index = cache_index // CB
        matches = block_index[:, None] == jnp.arange(blocks_all, dtype=jnp.int32)[None, :]
        kept = jnp.sum(jnp.where(matches, keep_row[None, :], 0), axis=1)
        visible = (cache_index < length) & (kept == 1)
        best_old, sums_old, mixed_old = running_now
        scores = (
            jnp.einsum("pqkgd,ckd->pkgqc", q_rot, key_rows, preferred_element_type=jnp.float32)
            * inv_root
        )
        scores = jnp.where(visible, scores, -jnp.inf)
        best_new = jnp.maximum(best_old, jnp.max(scores, axis=-1))
        weights = jnp.where(visible, jnp.exp(scores - best_new[..., None]), 0.0)
        factor = jnp.exp(best_old - best_new)
        sums_new = sums_old * factor + jnp.sum(weights, axis=-1)
        mixed_new = mixed_old * factor[..., None] + jnp.einsum(
            "pkgqc,ckd->pkgqd",
            weights.astype(jnp.bfloat16),
            value_block,
            preferred_element_type=jnp.float32,
        )
        return ((best_new, sums_new, mixed_new), None)

    result, ignored = lax.scan(visit, running, (key_blocks, value_blocks, block_starts))
    running = result
    highest, totals, mixture = running
    attended = mixture / totals[..., None]
    attended = (
        jnp.transpose(attended, (0, 3, 1, 2, 4))
        .reshape(2 * block_rows, local_q * HD)
        .astype(jnp.bfloat16)
    )
    return (attended[:block_rows], attended[block_rows:])


def solution(mesh):
    return jax.shard_map(
        local,
        mesh=mesh,
        in_specs=(
            P("blk", "tp"),
            P("blk", "tp"),
            P("blk"),
            P("blk"),
            P("blk", None),
            P(),
            P("blk", "tp"),
            P("tp"),
            P("blk", "tp"),
            P("tp"),
            P("blk", "tp"),
            P("tp"),
            P("blk", "tp"),
            P("blk", "tp"),
        ),
        out_specs=(P("blk", "tp"), P("blk", "tp")),
        check_vma=False,
    )
```

profile of v0, /device:TPU:59, one launch (start us, length us, event | category | flops | bytes accessed | tf_op | source)
XLA Modules:
  0.0 1078.7 jit_solution(2611596930218597881)
XLA Ops:
  16.3 62.3 %all-gather.8.cloned.1.call-done = bf16[128,5120]{1,0:T(8,128)(2,1)} async-done(((bf16[128,640]{1,0:T(8,128)(2,1)}), bf16[128,5120]{1,0:T(8,128)(2,1)}) %all-gather.8.cloned.1.call-update) | async-done | bytes 1310736 | tf_op jit(solution)/shard_map/all_gather | solution.py:56
  78.6 69.6 %all-gather.10.cloned.1.call-done = bf16[128,5120]{1,0:T(8,128)(2,1)} async-done(((bf16[128,640]{1,0:T(8,128)(2,1)}), bf16[128,5120]{1,0:T(8,128)(2,1)}) %all-gather.10.cloned.1.call-update) | async-done | bytes 1310736 | tf_op jit(solution)/shard_map/all_gather | solution.py:57
  148.2 1.9 broadcast_select_fusion
  150.8 121.0 %all-gather.12.cloned.1.call-done = bf16[5120,128]{1,0:T(8,128)(2,1)} async-done(((bf16[80,128]{1,0:T(8,128)(2,1)}), bf16[5120,128]{1,0:T(8,128)(2,1)}) %all-gather.12.cloned.1.call-update) | async-done | bytes 1310736 | tf_op jit(solution)/shard_map/all_gather | solution.py:63
  271.8 2.3 convolution_add_fusion.2
  274.2 115.1 %all-gather.16.cloned.1.call-done = bf16[5120,128]{1,0:T(8,128)(2,1)} async-done(((bf16[80,128]{1,0:T(8,128)(2,1)}), bf16[5120,128]{1,0:T(8,128)(2,1)}) %all-gather.16.cloned.1.call-update) | async-done | bytes 1310736 | tf_op jit(solution)/shard_map/all_gather | solution.py:64
  389.3 2.9 fusion.24
  392.2 120.2 %all-gather.14.cloned.1.call-done = bf16[5120,640]{1,0:T(8,128)(2,1)} async-done(((bf16[80,640]{1,0:T(8,128)(2,1)}), bf16[5120,640]{1,0:T(8,128)(2,1)}) %all-gather.14.cloned.1.call-update) | async-done | bytes 6553616 | tf_op jit(solution)/shard_map/all_gather | solution.py:62
  512.4 5.1 convolution_add_fusion
  519.3 109.8 %all-gather.18.cloned.1.call-done = bf16[4096,128]{1,0:T(8,128)(2,1)} async-done(((bf16[64,128]{1,0:T(8,128)(2,1)}), bf16[4096,128]{1,0:T(8,128)(2,1)}) %all-gather.18.cloned.1.call-update) | async-done | bytes 1048592 | tf_op jit(solution)/shard_map/all_gather | solution.py:95
  629.1 116.8 %all-gather.20.cloned.1.call-done = bf16[4096,128]{1,0:T(8,128)(2,1)} async-done(((bf16[64,128]{1,0:T(8,128)(2,1)}), bf16[4096,128]{1,0:T(8,128)(2,1)}) %all-gather.20.cloned.1.call-update) | async-done | bytes 1048592 | tf_op jit(solution)/shard_map/all_gather | solution.py:96
  745.8 324.3 %while.16 = (s32[]{:T(128)}, f32[2,1,5,128]{3,2,0,1:T(8,128)S(1)}, f32[2,1,5,128]{3,2,0,1:T(8,128)S(1)}, f32[2,1,5,128,128]{3,4,2,0,1:T(8,128)S(1)}, s32[64]{0:T...) while((s32[]{:T(128)}, f32[2,1,5,128]{3,2,0,1:T(8,128)S(1)}, ...), condition=%wide.region_7.8_spmd, body=%wide.region_3.7_spmd.sunk | while | flops 43025344 | bytes 2738821 | solution.py:129
  747.3 1.3 compare_and_fusion.2
  752.3 1.3 compare_and_fusion.2
  757.4 1.3 compare_and_fusion.2
  762.5 1.3 compare_and_fusion.2
  767.5 1.3 compare_and_fusion.2
  772.6 1.3 compare_and_fusion.2
  777.7 1.3 compare_and_fusion.2
  782.7 1.3 compare_and_fusion.2
  787.8 1.3 compare_and_fusion.2
  792.9 1.3 compare_and_fusion.2
  797.9 1.3 compare_and_fusion.2
  803.0 1.3 compare_and_fusion.2
  808.1 1.3 compare_and_fusion.2
  813.1 1.3 compare_and_fusion.2
  818.2 1.3 compare_and_fusion.2
  868.9 1.3 compare_and_fusion.2
  884.1 1.3 compare_and_fusion.2
  944.9 1.3 compare_and_fusion.2
  960.1 1.3 compare_and_fusion.2
  1020.9 1.3 compare_and_fusion.2
  (665 shorter events, 306.2 us)
Async XLA Ops:
  7.2 71.4 %all-gather.8.cloned.1.call-start = ((), (), s32[]{:S(2)}) async-start(), calls=%async_computation | async-start | bytes 1474560 | tf_op jit(solution)/shard_map/all_gather | solution.py:56
  7.9 140.3 %all-gather.10.cloned.1.call-start = ((), (), s32[]{:S(2)}) async-start(), calls=%async_computation.1 | async-start | bytes 1474560 | tf_op jit(solution)/shard_map/all_gather | solution.py:57
  8.6 263.1 %all-gather.12.cloned.1.call-start = ((), (), s32[]{:S(2)}) async-start(), calls=%async_computation.2 | async-start | bytes 1331200 | tf_op jit(solution)/shard_map/all_gather | solution.py:63
  9.4 379.9 %all-gather.16.cloned.1.call-start = ((), (), s32[]{:S(2)}) async-start(), calls=%async_computation.4 | async-start | bytes 1331200 | tf_op jit(solution)/shard_map/all_gather | solution.py:64
  10.0 502.5 %all-gather.14.cloned.1.call-start = ((), (), s32[]{:S(2)}) async-start(), calls=%async_computation.3 | async-start | bytes 6656000 | tf_op jit(solution)/shard_map/all_gather | solution.py:62
  10.5 618.5 %all-gather.18.cloned.1.call-start = ((), (), s32[]{:S(2)}) async-start(), calls=%async_computation.5 | async-start | bytes 1064960 | tf_op jit(solution)/shard_map/all_gather | solution.py:95
  11.1 734.7 %all-gather.20.cloned.1.call-start = ((), (), s32[]{:S(2)}) async-start(), calls=%async_computation.6 | async-start | bytes 1064960 | tf_op jit(solution)/shard_map/all_gather | solution.py:96
  13.3 376.0 %copy-start.2 = (f32[5120]{0:T(1024)}, f32[5120]{0:T(1024)S(1)}, u32[]{:S(2)}) copy-start(f32[5120]{0:T(1024)S(1)} %convert_element_type.54) | copy-start | bytes 61444
  78.6 71.6 %copy-start = (bf16[128,5120]{1,0:T(8,128)(2,1)S(1)}, bf16[128,5120]{1,0:T(8,128)(2,1)}, u32[]{:S(2)}) copy-start(bf16[128,5120]{1,0:T(8,128)(2,1)} %all-gather.8.cloned.1.call-done) | copy-start | bytes 3932164
  518.0 1.0 copy-start.1
  518.3 227.6 %copy-start.3 = (s32[1,64]{1,0:T(1,128)S(1)}, s32[1,64]{1,0:T(1,128)}, u32[]{:S(2)}) copy-start(s32[1,64]{1,0:T(1,128)} %param.20) | copy-start | bytes 772
Sparse Core Ops, SparseCore 0:
  11.2 67.3 all-gather.7
  81.8 66.3 all-gather.9
  150.4 121.3 all-gather.11
  273.8 115.4 all-gather.15
  391.3 121.0 all-gather.13
  514.4 114.6 all-gather.17
  631.2 114.5 all-gather.19
where the time goes:
time: 1090 us; the launch traced here: 1080 us
  waiting for transfers between devices  719 us (66%)
  other arithmetic  152 us (14%)
  matrix products  149 us (14%)
  local copies, waits for them, and re-layouts  39.8 us (4%)
  between operations  14.9 us (1%)
    all_gather x1, waiting for transfers between devices, local(): lax.all_gather(w_key, 'blk', axis=0, tiled=True)  121 us
    all_gather x1, waiting for transfers between devices, local(): lax.all_gather(w_query, 'blk', axis=0, tiled=True)  120 us
    all_gather x1, waiting for transfers between devices, local(): value_piece = lax.all_gather(cache_values, 'blk', axis=0, tiled=True)  117 us
    all_gather x1, waiting for transfers between devices, local(): lax.all_gather(w_value, 'blk', axis=0, tiled=True)  115 us
    all_gather x1, waiting for transfers between devices, local(): key_piece = lax.all_gather(cache_keys, 'blk', axis=0, tiled=True)  110 us
    and x64, other arithmetic, visit(): visible = (cache_index < length) & (kept == 1)  83.6 us
    dot_general x64, matrix products, visit(): jnp.einsum('pkgqc,ckd->pkgqd', weights.astype(jnp.bfloat16), value_block,...  75.1 us
    all_gather x1, waiting for transfers between devices, local(): lax.all_gather(given_embeds, 'tp', axis=1, tiled=True)  69.6 us
  transfers between devices with their start and end apart: 7, of which 7 were waited for; matrix products, arithmetic and copies ran while one was open for 2% of the time, Pallas kernels for 0%

commit v1 on v0

--- a/solution.py
+++ b/solution.py
@@ -53,7 +53,9 @@
     blocks_all = block_keep.shape[1]
     inv_root = 1.0 / math.sqrt(HD)
     first_rows, given_rows = (
-        lax.all_gather(embeds, "tp", axis=1, tiled=True),
+        jnp.concatenate(
+            lax.all_to_all(jnp.stack([embeds] * lax.axis_size("tp")), "tp", 0, 0), axis=1
+        ),
         lax.all_gather(given_embeds, "tp", axis=1, tiled=True),
     )
     revised = jnp.where(accept[:, None] == 1, given_rows, first_rows)

time: 1090 us -> 1040 us (0.954)
  waiting for transfers between devices: 719 us -> 654 us
    all_gather x1 -> x0, waiting for transfers between devices: 62.3 us -> none  [local(): lax.all_gather(embeds, 'tp', axis=1, tiled=True)]
    all_gather x1, waiting for transfers between devices: 69.6 us -> 52.6 us  [local(): lax.all_gather(given_embeds, 'tp', axis=1, tiled=True)]
    all_to_all x0 -> x1, waiting for transfers between devices: none -> 16.9 us  [local(): lax.all_to_all(jnp.stack([embeds] * lax.axis_size('tp')), 'tp', 0, 0)]
where the time goes in v1:
time: 1040 us; the launch traced here: 1030 us
  waiting for transfers between devices  654 us (63%)
  matrix products  151 us (15%)
  other arithmetic  148 us (14%)
  local copies, waits for them, and re-layouts  44.4 us (4%)
  between operations  15 us (1%)
    all_gather x1, waiting for transfers between devices, local(): lax.all_gather(w_key, 'blk', axis=0, tiled=True)  121 us
    all_gather x1, waiting for transfers between devices, local(): lax.all_gather(w_query, 'blk', axis=0, tiled=True)  120 us
    all_gather x1, waiting for transfers between devices, local(): value_piece = lax.all_gather(cache_values, 'blk', axis=0, tiled=True)  117 us
    all_gather x1, waiting for transfers between devices, local(): lax.all_gather(w_value, 'blk', axis=0, tiled=True)  115 us
    all_gather x1, waiting for transfers between devices, local(): key_piece = lax.all_gather(cache_keys, 'blk', axis=0, tiled=True)  109 us
    and x64, other arithmetic, visit(): visible = (cache_index < length) & (kept == 1)  83.6 us
    dot_general x64, matrix products, visit(): jnp.einsum('pkgqc,ckd->pkgqd', weights.astype(jnp.bfloat16), value_block,...  75.1 us
    dot_general x64, matrix products, visit(): jnp.einsum('pqkgd,ckd->pkgqc', q_rot, key_rows, preferred_element_type=jn...  62.6 us
  transfers between devices with their start and end apart: 7, of which 7 were waited for; matrix products, arithmetic and copies ran while one was open for 2% of the time, Pallas kernels for 0%

profile of v1, /device:TPU:59, one launch (start us, length us, event | category | flops | bytes accessed | tf_op | source)
XLA Modules:
  0.0 1025.4 jit_solution(9416742520710609554)
XLA Ops:
  7.3 1.7 copy.49
  11.7 2.1 stack.2
  13.7 9.1 all-to-all-start
  24.5 16.9 %all-to-all-done = bf16[8,128,640]{2,1,0:T(8,128)(2,1)S(1)} async-done(((bf16[8,128,640]{2,1,0:T(8,128)(2,1)}), bf16[8,128,640]{2,1,0:T(8,128)(2,1)S(1)}, u32[]{:S(2)}, u32[]{:S(2)}) %all-to-all-start) | async-done | bytes 1310752 | tf_op jit(solution)/shard_map/all_to_all | solution.py:57
  42.2 52.6 %all-gather.7.cloned.1.call-done = bf16[128,5120]{0,1:T(8,128)(2,1)} async-done(((bf16[128,640]{0,1:T(8,128)(2,1)}), bf16[128,5120]{0,1:T(8,128)(2,1)}) %all-gather.7.cloned.1.call-update) | async-done | bytes 1310736 | tf_op jit(solution)/shard_map/all_gather | solution.py:59
  94.8 1.5 broadcast_select_fusion
  97.0 121.4 %all-gather.9.cloned.1.call-done = bf16[5120,128]{1,0:T(8,128)(2,1)} async-done(((bf16[80,128]{1,0:T(8,128)(2,1)}), bf16[5120,128]{1,0:T(8,128)(2,1)}) %all-gather.9.cloned.1.call-update) | async-done | bytes 1310736 | tf_op jit(solution)/shard_map/all_gather | solution.py:65
  218.4 3.0 convolution_add_fusion.2
  221.5 114.6 %all-gather.13.cloned.1.call-done = bf16[5120,128]{1,0:T(8,128)(2,1)} async-done(((bf16[80,128]{1,0:T(8,128)(2,1)}), bf16[5120,128]{1,0:T(8,128)(2,1)}) %all-gather.13.cloned.1.call-update) | async-done | bytes 1310736 | tf_op jit(solution)/shard_map/all_gather | solution.py:66
  336.0 3.6 fusion.24
  339.6 119.5 %all-gather.11.cloned.1.call-done = bf16[5120,640]{1,0:T(8,128)(2,1)} async-done(((bf16[80,640]{1,0:T(8,128)(2,1)}), bf16[5120,640]{1,0:T(8,128)(2,1)}) %all-gather.11.cloned.1.call-update) | async-done | bytes 6553616 | tf_op jit(solution)/shard_map/all_gather | solution.py:64
  459.2 5.6 convolution_add_fusion
  466.5 109.3 %all-gather.15.cloned.1.call-done = bf16[4096,128]{1,0:T(8,128)(2,1)} async-done(((bf16[64,128]{1,0:T(8,128)(2,1)}), bf16[4096,128]{1,0:T(8,128)(2,1)}) %all-gather.15.cloned.1.call-update) | async-done | bytes 1048592 | tf_op jit(solution)/shard_map/all_gather | solution.py:97
  575.8 116.6 %all-gather.17.cloned.1.call-done = bf16[4096,128]{1,0:T(8,128)(2,1)} async-done(((bf16[64,128]{1,0:T(8,128)(2,1)}), bf16[4096,128]{1,0:T(8,128)(2,1)}) %all-gather.17.cloned.1.call-update) | async-done | bytes 1048592 | tf_op jit(solution)/shard_map/all_gather | solution.py:98
  692.4 324.4 %while.16 = (s32[]{:T(128)}, f32[2,1,5,128]{3,2,0,1:T(8,128)S(1)}, f32[2,1,5,128]{3,2,0,1:T(8,128)S(1)}, f32[2,1,5,128,128]{3,4,2,0,1:T(8,128)S(1)}, s32[64]{0:T...) while((s32[]{:T(128)}, f32[2,1,5,128]{3,2,0,1:T(8,128)S(1)}, ...), condition=%wide.region_7.8_spmd, body=%wide.region_3.7_spmd.sunk | while | flops 43025344 | bytes 2738821 | solution.py:131
  693.9 1.3 compare_and_fusion.2
  698.9 1.3 compare_and_fusion.2
  704.0 1.3 compare_and_fusion.2
  709.1 1.3 compare_and_fusion.2
  714.1 1.3 compare_and_fusion.2
  719.2 1.3 compare_and_fusion.2
  724.3 1.3 compare_and_fusion.2
  729.3 1.3 compare_and_fusion.2
  734.4 1.3 compare_and_fusion.2
  739.5 1.3 compare_and_fusion.2
  744.5 1.3 compare_and_fusion.2
  749.6 1.3 compare_and_fusion.2
  754.7 1.3 compare_and_fusion.2
  790.2 1.3 compare_and_fusion.2
  820.6 1.3 compare_and_fusion.2
  932.1 1.3 compare_and_fusion.2
  962.5 1.3 compare_and_fusion.2
  (675 shorter events, 306.4 us)
Async XLA Ops:
  7.2 16.2 %copy-start.2 = (bf16[5120]{0:T(1024)(128)(2,1)S(1)}, bf16[5120]{0:T(1024)(128)(2,1)}, u32[]{:S(2)}) copy-start(bf16[5120]{0:T(1024)(128)(2,1)} %param.21) | copy-start | bytes 30724
  7.2 16.2 %copy-start.3 = (bf16[640]{0:T(1024)(128)(2,1)S(1)}, bf16[640]{0:T(1024)(128)(2,1)}, u32[]{:S(2)}) copy-start(bf16[640]{0:T(1024)(128)(2,1)} %param.23) | copy-start | bytes 3844
  7.2 16.9 %copy-start.4 = (bf16[128]{0:T(256)(128)(2,1)S(1)}, bf16[128]{0:T(256)(128)(2,1)}, u32[]{:S(2)}) copy-start(bf16[128]{0:T(256)(128)(2,1)} %param.25) | copy-start | bytes 772
  7.2 16.9 %copy-start.5 = (bf16[128]{0:T(256)(128)(2,1)S(1)}, bf16[128]{0:T(256)(128)(2,1)}, u32[]{:S(2)}) copy-start(bf16[128]{0:T(256)(128)(2,1)} %param.27) | copy-start | bytes 772
  7.2 17.0 %copy-start.6 = (s32[128]{0:T(128)S(1)}, s32[128]{0:T(128)}, u32[]{:S(2)}) copy-start(s32[128]{0:T(128)} %param.18) | copy-start | bytes 1540
  7.2 87.6 %all-gather.7.cloned.1.call-start = ((), (), s32[]{:S(2)}) async-start(), calls=%async_computation.1 | async-start | bytes 1474560 | tf_op jit(solution)/shard_map/all_gather | solution.py:59
  9.0 209.4 %all-gather.9.cloned.1.call-start = ((), (), s32[]{:S(2)}) async-start(), calls=%async_computation.2 | async-start | bytes 1331200 | tf_op jit(solution)/shard_map/all_gather | solution.py:65
  9.8 326.3 %all-gather.13.cloned.1.call-start = ((), (), s32[]{:S(2)}) async-start(), calls=%async_computation.4 | async-start | bytes 1331200 | tf_op jit(solution)/shard_map/all_gather | solution.py:66
  10.5 448.7 %all-gather.11.cloned.1.call-start = ((), (), s32[]{:S(2)}) async-start(), calls=%async_computation.3 | async-start | bytes 6656000 | tf_op jit(solution)/shard_map/all_gather | solution.py:64
  11.1 564.7 %all-gather.15.cloned.1.call-start = ((), (), s32[]{:S(2)}) async-start(), calls=%async_computation.5 | async-start | bytes 1064960 | tf_op jit(solution)/shard_map/all_gather | solution.py:97
  13.7 27.7 %all-to-all-start = ((bf16[8,128,640]{2,1,0:T(8,128)(2,1)}), bf16[8,128,640]{2,1,0:T(8,128)(2,1)S(1)}, u32[]{:S(2)}, u32[]{:S(2)}) async-start(bf16[8,128,640]{2,1,0:T(8,128)(2,1)} %stack.2), calls=%async_computation | async-start | bytes 2621440 | tf_op jit(solution)/shard_map/all_to_all | solution.py:57
  22.8 669.6 %all-gather.17.cloned.1.call-start = ((), (), s32[]{:S(2)}) async-start(), calls=%async_computation.6 | async-start | bytes 1064960 | tf_op jit(solution)/shard_map/all_gather | solution.py:98
  23.4 312.6 %copy-start.1 = (f32[5120]{0:T(1024)}, f32[5120]{0:T(1024)S(1)}, u32[]{:S(2)}) copy-start(f32[5120]{0:T(1024)S(1)} %convert_element_type.54) | copy-start | bytes 61444
  465.2 1.0 copy-start
  465.5 226.9 %copy-start.7 = (s32[1,64]{1,0:T(1,128)S(1)}, s32[1,64]{1,0:T(1,128)}, u32[]{:S(2)}) copy-start(s32[1,64]{1,0:T(1,128)} %param.20) | copy-start | bytes 772
Sparse Core Ops, SparseCore 0:
  11.8 82.9 all-gather.6
  96.9 121.3 all-gather.8
  220.5 115.4 all-gather.12
  338.0 121.0 all-gather.10
  461.2 114.6 all-gather.14
  577.8 114.5 all-gather.16
